TPU v7x, 256 devices: a whole 4x4x8 slice. The times are simulated.
256 devices in a mesh: nodes: 64 (over z, y, core), mp: 4 (over x).
Axes of the slice: x: 4, y: 4, z: 8, core: 2. Of those that a mesh axis runs over, the one named last changes fastest.
Arguments:
- event_feats: bfloat16 [65536, 512], P('nodes'), may hold values from -6 to 6
- event_owner: int32 [65536, 1], P('nodes'), may hold values from 0 to 63; in each aligned block of 1024 rows (0 to 1023, 1024 to 2047, ...) at most 32 rows name the same one
- event_slot: int32 [65536], P('nodes'), may hold values from 0 to 255
- memory: bfloat16 [16384, 1024], P('nodes'), may hold values from -6 to 6
- w_msg_event: bfloat16 [512, 2048], P(None, 'mp'), may hold values from -0.25 to 0.25
- w_msg_state: bfloat16 [1024, 2048], P(None, 'mp'), may hold values from -0.1875 to 0.1875
- b_msg: float32 [2048], P('mp'), may hold values from -3 to 3
- w_msg_out: bfloat16 [2048, 1024], P('mp'), may hold values from -0.125 to 0.125
- b_out: float32 [1024], replicated, may hold values from -3 to 3
- w_input: bfloat16 [3, 1024, 1024], P(None, None, 'mp'), may hold values from -0.1875 to 0.1875
- w_hidden: bfloat16 [3, 1024, 1024], P(None, None, 'mp'), may hold values from -0.1875 to 0.1875
- b_input: float32 [3, 1024], P(None, 'mp'), may hold values from -3 to 3
- b_hidden: float32 [3, 1024], P(None, 'mp'), may hold values from -3 to 3
- state_slots: int32 [4096, 32], P('nodes'), may hold values from 0 to 255
- neighbours: int32 [16384, 10], P('nodes'), may hold values from 0 to 2047
- query_slots: int32 [16384], P('nodes'), may hold values from 0 to 255
- w_neigh: bfloat16 [1024, 1024], P('mp'), may hold values from -0.1875 to 0.1875
- w_self: bfloat16 [1024, 1024], P('mp'), may hold values from -0.1875 to 0.1875
- b_embed: float32 [1024], replicated, may hold values from -3 to 3
Outputs:
- new_memory: bfloat16 [16384, 1024], P('nodes', 'mp')
- embedding: bfloat16 [16384, 1024], P(('nodes', 'mp'))
Inputs may be any that keep to these rules, and one draw needn't show every extreme that they name: `event_owner`: among the 1024 events of one block of events, at most 32 name the same owner, and in every draw some owner is named exactly 32 times by some block.
All inputs are finite; a program needn't handle non-finite values.
Results may differ from a plain program's by a relative error of at most 0.014.
Values may be sent and summed in bfloat16 or wider, within the bound.
No kernel may reach another device: no remote copies, remote signals or barrier semaphores. Data moves between devices by JAX's collectives and lax.ppermute only.
A program may use at most 64 MiB of HBM per device.

v0:
```python
import jax
import jax.numpy as jnp
from jax import lax
from jax.sharding import PartitionSpec as P


def per_device(
    event_feats,
    event_owner,
    event_slot,
    memory,
    w_msg_event,
    w_msg_state,
    b_msg,
    w_msg_out,
    b_out,
    w_input,
    w_hidden,
    b_input,
    b_hidden,
    state_slots,
    neighbours,
    query_slots,
    w_neigh,
    w_self,
    b_embed,
):
    owner_count = lax.axis_size("nodes")
    share_count = lax.axis_size("mp")
    mp_index = lax.axis_index("mp")
    event_rows = event_feats.shape[0]
    feat_width = event_feats.shape[1]
    mem_rows = memory.shape[0]
    mem_width = memory.shape[1]
    col_share = mem_width // share_count
    capacity = 2 * event_rows // owner_count
    owner = event_owner[:, 0]
    match = (owner[:, None] == lax.broadcasted_iota(jnp.int32, (1, owner_count), 1)).astype(
        jnp.int32
    )
    before = jnp.cumsum(match, axis=0) - match
    place = jnp.sum(before * match, axis=1)
    target = owner * capacity + place
    id_buffer = jnp.full((owner_count * capacity,), -1, jnp.int32).at[target].set(event_slot)
    id_buffer = id_buffer.reshape(owner_count, capacity)
    feat_buffer = (
        jnp.zeros((owner_count * capacity, feat_width), jnp.bfloat16).at[target].set(event_feats)
    )
    feat_buffer = feat_buffer.reshape(owner_count, capacity, feat_width)
    arrived = lax.all_to_all(feat_buffer, "nodes", split_axis=0, concat_axis=0, tiled=True)
    arrived_ids = lax.all_to_all(id_buffer, "nodes", split_axis=0, concat_axis=0, tiled=True)
    recv_rows = owner_count * capacity
    arrived = arrived.reshape(recv_rows, feat_width)
    arrived_ids = arrived_ids.reshape(recv_rows)
    valid = arrived_ids >= 0
    safe_ids = jnp.where(valid, arrived_ids, 0)
    segment_ids = jnp.where(valid, arrived_ids, mem_rows)
    state_proj = jnp.dot(memory, w_msg_state, preferred_element_type=jnp.float32)
    pre = (
        jnp.dot(arrived, w_msg_event, preferred_element_type=jnp.float32)
        + jnp.take(state_proj, safe_ids, axis=0)
        + b_msg
    )
    hidden_msg = jax.nn.relu(pre).astype(jnp.bfloat16)
    partial_msg = jnp.dot(hidden_msg, w_msg_out, preferred_element_type=jnp.float32)
    partial_total = jax.ops.segment_sum(partial_msg, segment_ids, num_segments=mem_rows + 1)[
        :mem_rows
    ]
    counts = jax.ops.segment_sum(valid.astype(jnp.float32), segment_ids, num_segments=mem_rows + 1)[
        :mem_rows
    ]
    divisor = jnp.maximum(counts, 1.0)[:, None]
    msg_total = lax.psum(partial_total.astype(jnp.bfloat16), "mp").astype(jnp.float32)
    aggregate = (msg_total / divisor + b_out).astype(jnp.bfloat16)
    gates_in = (
        jnp.einsum("nd,gdc->gnc", aggregate, w_input, preferred_element_type=jnp.float32)
        + b_input[:, None, :]
    )
    gates_st = (
        jnp.einsum("nd,gdc->gnc", memory, w_hidden, preferred_element_type=jnp.float32)
        + b_hidden[:, None, :]
    )
    reset_gate = jax.nn.sigmoid(gates_in[0] + gates_st[0])
    update_gate = jax.nn.sigmoid(gates_in[1] + gates_st[1])
    candidate = jnp.tanh(gates_in[2] + reset_gate * gates_st[2])
    old_state = lax.dynamic_slice_in_dim(memory, mp_index * col_share, col_share, 1).astype(
        jnp.float32
    )
    updated = (1.0 - update_gate) * candidate + update_gate * old_state
    new_memory = jnp.where((counts > 0.0)[:, None], updated, old_state).astype(jnp.bfloat16)
    outgoing = jnp.take(new_memory, state_slots, axis=0)
    relayed = lax.all_to_all(outgoing, "nodes", split_axis=0, concat_axis=0, tiled=True)
    relayed = relayed.reshape(relayed.shape[0] * relayed.shape[1], col_share)
    neigh_rows = jnp.take(relayed, neighbours, axis=0).astype(jnp.float32)
    neigh_mean = (jnp.sum(neigh_rows, axis=1) / neighbours.shape[1]).astype(jnp.bfloat16)
    self_state = jnp.take(new_memory, query_slots, axis=0)
    summed = lax.psum_scatter(
        (
            jnp.dot(neigh_mean, w_neigh, preferred_element_type=jnp.float32)
            + jnp.dot(self_state, w_self, preferred_element_type=jnp.float32)
        ).astype(jnp.bfloat16),
        "mp",
        scatter_dimension=0,
        tiled=True,
    ).astype(jnp.float32)
    embedding = jax.nn.relu(summed + b_embed).astype(jnp.bfloat16)
    return (new_memory, embedding)


def solution(mesh):
    in_specs = (
        P("nodes", None),
        P("nodes", None),
        P("nodes"),
        P("nodes", None),
        P(None, "mp"),
        P(None, "mp"),
        P("mp"),
        P("mp", None),
        P(),
        P(None, None, "mp"),
        P(None, None, "mp"),
        P(None, "mp"),
        P(None, "mp"),
        P("nodes", None),
        P("nodes", None),
        P("nodes"),
        P("mp", None),
        P("mp", None),
        P(),
    )
    out_specs = (P("nodes", "mp"), P(("nodes", "mp"), None))
    return jax.shard_map(
        per_device, mesh=mesh, in_specs=in_specs, out_specs=out_specs, check_vma=False
    )
```

profile of v0, /device:TPU:8, one launch (start us, length us, event | category | flops | bytes accessed | tf_op | source)
XLA Modules:
  0.0 281.5 jit_solution(5040244256541828532)
XLA Ops:
  7.2 0.8 fusion.31
  8.0 18.0 %reduce-window.6 = s32[64,8,128]{2,1,0:T(8,128)S(1)} reduce-window(s32[64,8,128]{2,1,0:T(8,128)S(1)} %fusion.31, s32[]{:T(128)} %constant.48.clone.1), window={size=1x1x128 pad=0_0x0_0x127_0}, to_apply=%region_0.0 | reduce-window | flops 8323072 | bytes 524292 | tf_op jit(solution)/shard_map/reduce-window
  26.0 0.1 slice.49
  26.2 0.1 copy.33
  26.4 0.1 copy.34
  26.4 0.1 broadcast_add_fusion
  26.6 0.1 fusion.17
  26.7 4.5 %scatter_custom_fusion = s32[2048]{0:T(1024)S(1)} fusion(s32[1024]{0:T(1024)S(1)} %bitcast.71, s32[1024]{0:T(1024)} %param.21, s32[]{:T(128)} %constant.46.clone.1), kind=kCustom, calls=%fused_computation.79 | custom fusion | bytes 8704 | tf_op jit(solution)/shard_map/scatter | solution.py:44
  31.2 0.7 all_to_all.12
  31.9 12.1 %all-to-all-start = ((s32[64,1,32]{2,1,0:T(1,128)}), s32[64,1,32]{2,1,0:T(1,128)S(1)}, u32[]{:S(2)}, u32[]{:S(2)}) async-start(s32[64,1,32]{2,1,0:T(1,128)} %bitcast.6), calls=%async_computation | async-start | bytes 65536 | tf_op jit(solution)/shard_map/all_to_all | solution.py:51
  44.0 7.2 %scatter_custom_fusion.2 = bf16[2048,512]{1,0:T(8,128)(2,1)} fusion(s32[1024]{0:T(1024)S(1)} %bitcast.72, bf16[1024,512]{1,0:T(8,128)(2,1)} %param.19, bf16[]{:T(256)} %constant.58.clone.1), kind=kCustom, calls=%fused_computation.18 | custom fusion | bytes 2097664 | tf_op jit(solution)/shard_map/scatter | solution.py:47
  51.2 1.4 all-to-all-done
  52.5 9.3 %all-to-all-start.1 = ((bf16[64,32,512]{2,1,0:T(8,128)(2,1)}), bf16[64,32,512]{2,1,0:T(8,128)(2,1)}, u32[]{:S(2)}, u32[]{:S(2)}) async-start(bf16[64,32,512]{2,1,0:T(8,128)(2,1)} %bitcast.60), calls=%async_computation.1 | async-start | bytes 4194304 | tf_op jit(solution)/shard_map/all_to_all | solution.py:50
  61.8 0.2 all-reduce.2.cloned.1.call-start
  62.1 0.1 copy.40
  62.1 0.1 reshape.145
  62.2 1.5 fusion.45
  63.7 1.6 fusion.1
  65.4 0.5 broadcast.139
  65.9 0.7 reduce.5
  66.6 0.1 reshape.123
  66.7 0.1 reshape.124
  66.8 9.0 %gather_fusion = f32[2048,512]{1,0:T(8,128)} fusion(f32[256,512]{1,0:T(8,128)S(1)} %fusion.45, s32[2048]{0:T(1024)S(1)} %broadcast_clamp_fusion.1), kind=kCustom, calls=%fused_computation | custom fusion | bytes 8396800 | tf_op jit(solution)/shard_map/jit(_take)/gather | solution.py:61
  75.8 37.1 %all-to-all-done.1 = bf16[64,32,512]{2,1,0:T(8,128)(2,1)} async-done(((bf16[64,32,512]{2,1,0:T(8,128)(2,1)}), bf16[64,32,512]{2,1,0:T(8,128)(2,1)}, u32[]{:S(2)}, u32[]{:S(2)}) %all-to-all-start.1) | async-done | bytes 2097184 | tf_op jit(solution)/shard_map/all_to_all | solution.py:50
  113.0 7.9 %fusion.5 = f32[2048,1024]{1,0:T(8,128)} fusion(bf16[512,1024]{1,0:T(8,128)(2,1)} %param.26, f32[2048,512]{1,0:T(8,128)} %gather_fusion, bf16[2048,512]{1,0:T(8,128)(2,1)} %bitcast.9, bf16[512,512]{1,0:T(8,128)(2,1)S(1)} %copy-done.10, f32[512]{0:T(512)S(1)} %copy-done.14, pred[2048]{0:T(1024)(128)(4,1)S(1)} %get-tuple-element.3), kind=kOutput, calls=%fused_computation.21 | convolution fusion | flops 3226468352 | bytes 16257024 | tf_op jit(solution)/shard_map/dot_general | solution.py:65
  120.8 19.2 %scatter_custom_fusion.3 = f32[257,1024]{1,0:T(8,128)S(1)} fusion(s32[2048]{0:T(1024)S(1)} %bitcast.69, f32[2048,1024]{1,0:T(8,128)} %fusion.5, f32[]{:T(128)} %constant.39.clone.1), kind=kCustom, calls=%fused_computation.22 | custom fusion | flops 2097152 | bytes 1053184 | tf_op jit(solution)/shard_map/scatter-add | solution.py:66
  140.1 0.9 slice.101
  141.0 0.1 copy.39
  141.1 14.7 %scatter_custom_fusion.1 = f32[257]{0:T(512)S(1)} fusion(s32[2048]{0:T(1024)S(1)} %bitcast.70, f32[2048]{0:T(1024)S(1)} %get-tuple-element.2, f32[]{:T(128)} %constant.39.clone.1), kind=kCustom, calls=%fused_computation.83 | custom fusion | flops 2048 | bytes 1032 | tf_op jit(solution)/shard_map/scatter-add | solution.py:69
  155.8 29.8 %all-reduce.2.cloned.1.call-done = bf16[256,1024]{1,0:T(8,128)(2,1)} async-done(((bf16[256,1024]{1,0:T(8,128)(2,1)}), bf16[256,1024]{1,0:T(8,128)(2,1)}) %all-reduce.2.cloned.1.call-update) | async-done | bytes 524304 | tf_op jit(solution)/shard_map/psum | solution.py:73
  185.6 2.2 fusion.2
  187.8 1.1 fusion.14
  188.9 7.5 %gather_fusion.1 = bf16[2048,256]{1,0:T(8,128)(2,1)S(1)} fusion(bf16[256,256]{1,0:T(8,128)(2,1)S(1)} %fusion.14, s32[2048]{0:T(1024)S(1)} %broadcast_clamp_fusion), kind=kCustom, calls=%fused_computation.1 | custom fusion | bytes 2105344 | tf_op jit(solution)/shard_map/jit(_take)/gather | solution.py:91
  196.4 1.3 broadcast_select_fusion
  197.7 10.6 %all-to-all-start.2 = ((bf16[64,32,256]{2,1,0:T(8,128)(2,1)}), bf16[64,32,256]{2,1,0:T(8,128)(2,1)S(1)}, u32[]{:S(2)}, u32[]{:S(2)}) async-start(bf16[64,32,256]{2,1,0:T(8,128)(2,1)} %broadcast_select_fusion), calls=%async_computation.2 | async-start | bytes 2097152 | tf_op jit(solution)/shard_map/all_to_all | solution.py:92
  208.3 0.3 reduce-scatter.2.cloned.1.call-start
  208.6 0.1 copy.41
  208.7 0.1 reshape.153
  208.8 0.1 copy.38
  209.0 1.2 gather_fusion.3
  210.2 26.8 %all-to-all-done.2 = bf16[64,32,256]{2,1,0:T(8,128)(2,1)S(1)} async-done(((bf16[64,32,256]{2,1,0:T(8,128)(2,1)}), bf16[64,32,256]{2,1,0:T(8,128)(2,1)S(1)}, u32[]{:S(2)}, u32[]{:S(2)}) %all-to-all-start.2) | async-done | bytes 1048608 | tf_op jit(solution)/shard_map/all_to_all | solution.py:92
  237.0 8.1 %gather_fusion.2 = bf16[2560,256]{1,0:T(8,128)(2,1)} fusion(bf16[2048,256]{1,0:T(8,128)(2,1)S(1)} %bitcast.59, s32[3072]{0:T(1024)S(1)} %pad_clamp_fusion), kind=kCustom, calls=%fused_computation.2 | custom fusion | bytes 2631680 | tf_op jit(solution)/shard_map/jit(_take)/gather | solution.py:94
  245.2 3.6 %reshape.152 = bf16[256,10,256]{2,1,0:T(8,128)(2,1)} reshape(bf16[2560,256]{1,0:T(8,128)(2,1)} %gather_fusion.2) | data formatting | bytes 2621440 | tf_op jit(solution)/shard_map/jit(_take)/gather | solution.py:94
  248.8 2.7 convert_reduce_fusion
  251.6 0.3 fusion.32
  251.9 1.1 fusion
  253.1 20.0 %reduce-scatter.2.cloned.1.call-done = bf16[64,1024]{1,0:T(8,128)(2,1)} async-done(((bf16[256,1024]{1,0:T(8,128)(2,1)}), bf16[64,1024]{1,0:T(8,128)(2,1)}) %reduce-scatter.2.cloned.1.call-update) | async-done | bytes 131088 | tf_op jit(solution)/shard_map/reduce_scatter | solution.py:97
  273.0 1.6 maximum_convert_fusion.1
  (49 shorter events, 0.3 us)
Async XLA Ops:
  7.2 56.6 %copy-start = (bf16[3,1024,256]{2,1,0:T(8,128)(2,1)S(1)}, bf16[3,1024,256]{2,1,0:T(8,128)(2,1)}, u32[]{:S(2)}) copy-start(bf16[3,1024,256]{2,1,0:T(8,128)(2,1)} %param.29) | copy-start | bytes 4718596
  7.2 19.4 %copy-start.7 = (s32[1024,1]{0,1:T(1,128)S(1)}, s32[1024,1]{0,1:T(1,128)}, u32[]{:S(2)}) copy-start(s32[1024,1]{0,1:T(1,128)} %param.20) | copy-start | bytes 12292
  31.9 20.7 %all-to-all-start = ((s32[64,1,32]{2,1,0:T(1,128)}), s32[64,1,32]{2,1,0:T(1,128)S(1)}, u32[]{:S(2)}, u32[]{:S(2)}) async-start(s32[64,1,32]{2,1,0:T(1,128)} %bitcast.6), calls=%async_computation | async-start | bytes 65536 | tf_op jit(solution)/shard_map/all_to_all | solution.py:51
  52.5 9.5 %copy-start.5 = (s32[64,32]{0,1:T(8,128)S(1)}, s32[64,32]{0,1:T(8,128)}, u32[]{:S(2)}) copy-start(s32[64,32]{0,1:T(8,128)} %param.32) | copy-start | bytes 24580
  52.5 9.7 %copy-start.2 = (bf16[1024,512]{1,0:T(8,128)(2,1)S(1)}, bf16[1024,512]{1,0:T(8,128)(2,1)}, u32[]{:S(2)}) copy-start(bf16[1024,512]{1,0:T(8,128)(2,1)} %param.24) | copy-start | bytes 3145732
  52.5 60.4 %all-to-all-start.1 = ((bf16[64,32,512]{2,1,0:T(8,128)(2,1)}), bf16[64,32,512]{2,1,0:T(8,128)(2,1)}, u32[]{:S(2)}, u32[]{:S(2)}) async-start(bf16[64,32,512]{2,1,0:T(8,128)(2,1)} %bitcast.60), calls=%async_computation.1 | async-start | bytes 4194304 | tf_op jit(solution)/shard_map/all_to_all | solution.py:50
  61.8 1.9 copy-start.11
  61.8 123.8 %all-reduce.2.cloned.1.call-start = ((), (), s32[]{:S(2)}) async-start(), calls=%async_computation.4 | async-start | bytes 1048576 | tf_op jit(solution)/shard_map/psum | solution.py:73
  66.8 46.1 %copy-start.10 = (bf16[512,512]{1,0:T(8,128)(2,1)S(1)}, bf16[512,512]{1,0:T(8,128)(2,1)}, u32[]{:S(2)}) copy-start(bf16[512,512]{1,0:T(8,128)(2,1)} %param.23) | copy-start | bytes 1572868
  66.8 46.1 %copy-start.14 = (f32[512]{0:T(512)S(1)}, f32[512]{0:T(512)}, u32[]{:S(2)}) copy-start(f32[512]{0:T(512)} %param.25) | copy-start | bytes 6148
  120.8 64.7 %copy-start.12 = (f32[1024]{0:T(1024)S(1)}, f32[1024]{0:T(1024)}, u32[]{:S(2)}) copy-start(f32[1024]{0:T(1024)} %param.27) | copy-start | bytes 12292
  120.8 64.7 %copy-start.13 = (f32[3,256]{1,0:T(4,128)S(1)}, f32[3,256]{1,0:T(4,128)}, u32[]{:S(2)}) copy-start(f32[3,256]{1,0:T(4,128)} %param.30) | copy-start | bytes 9220
  188.9 20.1 %copy-start.1 = (bf16[256,256]{1,0:T(8,128)(2,1)}, bf16[256,256]{1,0:T(8,128)(2,1)S(1)}, u32[]{:S(2)}) copy-start(bf16[256,256]{1,0:T(8,128)(2,1)S(1)} %fusion.14) | copy-start | bytes 393220
  196.4 12.1 %copy-start.6 = (s32[256,10]{0,1:T(8,128)S(1)}, s32[256,10]{0,1:T(8,128)}, u32[]{:S(2)}) copy-start(s32[256,10]{0,1:T(8,128)} %param.33) | copy-start | bytes 30724
  196.4 12.5 %copy-start.9 = (s32[256]{0:T(256)S(1)}, s32[256]{0:T(256)}, u32[]{:S(2)}) copy-start(s32[256]{0:T(256)} %param.34) | copy-start | bytes 3076
  197.7 39.3 %all-to-all-start.2 = ((bf16[64,32,256]{2,1,0:T(8,128)(2,1)}), bf16[64,32,256]{2,1,0:T(8,128)(2,1)S(1)}, u32[]{:S(2)}, u32[]{:S(2)}) async-start(bf16[64,32,256]{2,1,0:T(8,128)(2,1)} %broadcast_select_fusion), calls=%async_computation.2 | async-start | bytes 2097152 | tf_op jit(solution)/shard_map/all_to_all | solution.py:92
  208.3 64.8 %reduce-scatter.2.cloned.1.call-start = ((), (), s32[]{:S(2)}) async-start(), calls=%async_computation.5 | async-start | bytes 655360 | tf_op jit(solution)/shard_map/reduce_scatter | solution.py:97
  245.2 6.4 %copy-start.3 = (bf16[256,1024]{1,0:T(8,128)(2,1)S(1)}, bf16[256,1024]{1,0:T(8,128)(2,1)}, u32[]{:S(2)}) copy-start(bf16[256,1024]{1,0:T(8,128)(2,1)} %param.35) | copy-start | bytes 1572868
  248.8 3.1 %copy-start.4 = (bf16[256,1024]{1,0:T(8,128)(2,1)S(1)}, bf16[256,1024]{1,0:T(8,128)(2,1)}, u32[]{:S(2)}) copy-start(bf16[256,1024]{1,0:T(8,128)(2,1)} %param.36) | copy-start | bytes 1572868
  251.6 21.5 %copy-start.8 = (f32[1024]{0:T(1024)S(1)}, f32[1024]{0:T(1024)}, u32[]{:S(2)}) copy-start(f32[1024]{0:T(1024)} %param.37) | copy-start | bytes 12292
Sparse Core Ops, SparseCore 0:
  141.1 44.4 all-reduce.1
  253.2 19.7 reduce-scatter.1
where the time goes:
time: 282 us; the launch traced here: 281 us
  waiting for transfers between devices  115 us (41%)
  other arithmetic  60.5 us (21%)
  local copies, waits for them, and re-layouts  44.4 us (16%)
  starting transfers between devices  32.4 us (11%)
  matrix products  14.6 us (5%)
  between operations  14.5 us (5%)
    all_to_all x1, waiting for transfers between devices, per_device(): lax.all_to_all(feat_buffer, 'nodes', split_axis=0, concat_axis=0, tiled=T...  37.1 us
    psum x1, waiting for transfers between devices, per_device(): lax.psum(partial_total.astype(jnp.bfloat16), 'mp').astype(jnp.float32)  29.8 us
    all_to_all x1, waiting for transfers between devices, per_device(): lax.all_to_all(outgoing, 'nodes', split_axis=0, concat_axis=0, tiled=True)  26.8 us
    reduce_scatter x1, waiting for transfers between devices, per_device(): lax.psum_scatter((jnp.dot(neigh_mean, w_neigh, preferred_element_type=jnp...  20 us
    scatter-add x1, other arithmetic, per_device(): jax.ops.segment_sum(partial_msg, segment_ids, num_segments=mem_rows + 1)  19.2 us
    another operation x3, other arithmetic  18.2 us
    scatter-add x1, other arithmetic, per_device(): jax.ops.segment_sum(valid.astype(jnp.float32), segment_ids, num_segments=...  14.7 us
    all_to_all x1, starting transfers between devices, per_device(): lax.all_to_all(id_buffer, 'nodes', split_axis=0, concat_axis=0, tiled=True)  12.1 us
  transfers between devices with their start and end apart: 5, of which 5 were waited for; matrix products, arithmetic and copies ran while one was open for 13% of the time, Pallas kernels for 0%

commit v1 on v0

--- a/solution.py
+++ b/solution.py
@@ -1,7 +1,16 @@
+import functools
 import jax
 import jax.numpy as jnp
 from jax import lax
 from jax.sharding import PartitionSpec as P
+
+
+def groups_meet(my_data, along_axis):
+    prior = jnp.sum(lax.all_gather(my_data, axis_name=along_axis), axis=0)
+    return prior
+
+
+group_patch = functools.partial(groups_meet, along_axis="mp")
 
 
 def per_device(
@@ -70,7 +79,7 @@
         :mem_rows
     ]
     divisor = jnp.maximum(counts, 1.0)[:, None]
-    msg_total = lax.psum(partial_total.astype(jnp.bfloat16), "mp").astype(jnp.float32)
+    msg_total = group_patch(partial_total.astype(jnp.bfloat16)).astype(jnp.float32)
     aggregate = (msg_total / divisor + b_out).astype(jnp.bfloat16)
     gates_in = (
         jnp.einsum("nd,gdc->gnc", aggregate, w_input, preferred_element_type=jnp.float32)

time: 282 us -> 269 us (0.954)
  waiting for transfers between devices: 115 us -> 101 us
    psum x1 -> x0, waiting for transfers between devices: 29.8 us -> none  [per_device(): lax.psum(partial_total.astype(jnp.bfloat16), 'mp').astype(jnp.float32)]
    all_gather x0 -> x1, waiting for transfers between devices: none -> 14.1 us  [groups_meet(): prior = jnp.sum(lax.all_gather(my_data, axis_name=along_axis), axis=0)]
    reduce_sum x0 -> x1, other arithmetic: none -> 2.93 us  [groups_meet(): prior = jnp.sum(lax.all_gather(my_data, axis_name=along_axis), axis=0)]
where the time goes in v1:
time: 269 us; the launch traced here: 268 us
  waiting for transfers between devices  101 us (38%)
  other arithmetic  62.6 us (23%)
  local copies, waits for them, and re-layouts  44.4 us (17%)
  starting transfers between devices  32.4 us (12%)
  between operations  14.5 us (5%)
  matrix products  13.4 us (5%)
    all_to_all x1, waiting for transfers between devices, per_device(): lax.all_to_all(feat_buffer, 'nodes', split_axis=0, concat_axis=0, tiled=T...  39 us
    all_to_all x1, waiting for transfers between devices, per_device(): lax.all_to_all(outgoing, 'nodes', split_axis=0, concat_axis=0, tiled=True)  26.8 us
    reduce_scatter x1, waiting for transfers between devices, per_device(): lax.psum_scatter((jnp.dot(neigh_mean, w_neigh, preferred_element_type=jnp...  19.5 us
    scatter-add x1, other arithmetic, per_device(): jax.ops.segment_sum(partial_msg, segment_ids, num_segments=mem_rows + 1)  19.3 us
    another operation x3, other arithmetic  18.2 us
    scatter-add x1, other arithmetic, per_device(): jax.ops.segment_sum(valid.astype(jnp.float32), segment_ids, num_segments=...  14.7 us
    all_gather x1, waiting for transfers between devices, groups_meet(): prior = jnp.sum(lax.all_gather(my_data, axis_name=along_axis), axis=0)  14.1 us
    all_to_all x1, starting transfers between devices, per_device(): lax.all_to_all(id_buffer, 'nodes', split_axis=0, concat_axis=0, tiled=True)  12.1 us
  transfers between devices with their start and end apart: 5, of which 5 were waited for; matrix products, arithmetic and copies ran while one was open for 13% of the time, Pallas kernels for 0%

profile of v1, /device:TPU:8, one launch (start us, length us, event | category | flops | bytes accessed | tf_op | source)
XLA Modules:
  0.0 268.0 jit_solution(11205271239898431010)
XLA Ops:
  7.2 0.8 fusion.31
  8.0 18.0 %reduce-window.6 = s32[64,8,128]{2,1,0:T(8,128)S(1)} reduce-window(s32[64,8,128]{2,1,0:T(8,128)S(1)} %fusion.31, s32[]{:T(128)} %constant.49.clone.1), window={size=1x1x128 pad=0_0x0_0x127_0}, to_apply=%region_0.0 | reduce-window | flops 8323072 | bytes 524292 | tf_op jit(solution)/shard_map/reduce-window
  26.0 0.1 slice.49
  26.2 0.1 copy.42
  26.4 0.1 copy.43
  26.4 0.1 broadcast_add_fusion
  26.7 4.5 %scatter_custom_fusion = s32[2048]{0:T(1024)S(1)} fusion(s32[1024]{0:T(1024)S(1)} %bitcast.73, s32[1024]{0:T(1024)} %param.21, s32[]{:T(128)} %constant.47.clone.1), kind=kCustom, calls=%fused_computation.79 | custom fusion | bytes 8704 | tf_op jit(solution)/shard_map/scatter | solution.py:53
  31.2 0.7 all_to_all.12
  31.9 12.1 %all-to-all-start = ((s32[64,1,32]{2,1,0:T(1,128)}), s32[64,1,32]{2,1,0:T(1,128)S(1)}, u32[]{:S(2)}, u32[]{:S(2)}) async-start(s32[64,1,32]{2,1,0:T(1,128)} %bitcast.6), calls=%async_computation | async-start | bytes 65536 | tf_op jit(solution)/shard_map/all_to_all | solution.py:60
  44.0 7.2 %scatter_custom_fusion.2 = bf16[2048,512]{1,0:T(8,128)(2,1)} fusion(s32[1024]{0:T(1024)S(1)} %bitcast.74, bf16[1024,512]{1,0:T(8,128)(2,1)} %param.19, bf16[]{:T(256)} %constant.59.clone.1), kind=kCustom, calls=%fused_computation.18 | custom fusion | bytes 2097664 | tf_op jit(solution)/shard_map/scatter | solution.py:56
  51.2 1.4 all-to-all-done
  52.5 9.3 %all-to-all-start.1 = ((bf16[64,32,512]{2,1,0:T(8,128)(2,1)}), bf16[64,32,512]{2,1,0:T(8,128)(2,1)}, u32[]{:S(2)}, u32[]{:S(2)}) async-start(bf16[64,32,512]{2,1,0:T(8,128)(2,1)} %bitcast.61), calls=%async_computation.1 | async-start | bytes 4194304 | tf_op jit(solution)/shard_map/all_to_all | solution.py:59
  61.8 0.2 all-gather.3.cloned.1.call-start
  62.0 1.5 fusion.45
  63.5 0.5 broadcast.139
  64.0 0.7 reduce.6
  64.8 0.1 reshape.123
  64.8 0.1 reshape.124
  65.0 9.0 %gather_fusion = f32[2048,512]{1,0:T(8,128)} fusion(f32[256,512]{1,0:T(8,128)S(1)} %fusion.45, s32[2048]{0:T(1024)S(1)} %broadcast_clamp_fusion.1), kind=kCustom, calls=%fused_computation | custom fusion | bytes 8396800 | tf_op jit(solution)/shard_map/jit(_take)/gather | solution.py:70
  73.9 39.0 %all-to-all-done.1 = bf16[64,32,512]{2,1,0:T(8,128)(2,1)} async-done(((bf16[64,32,512]{2,1,0:T(8,128)(2,1)}), bf16[64,32,512]{2,1,0:T(8,128)(2,1)}, u32[]{:S(2)}, u32[]{:S(2)}) %all-to-all-start.1) | async-done | bytes 2097184 | tf_op jit(solution)/shard_map/all_to_all | solution.py:59
  112.9 7.7 %fusion.5 = f32[2048,1024]{1,0:T(8,128)} fusion(bf16[512,1024]{1,0:T(8,128)(2,1)S(1)} %copy-done.11, f32[2048,512]{1,0:T(8,128)} %gather_fusion, bf16[2048,512]{1,0:T(8,128)(2,1)} %bitcast.9, bf16[512,512]{1,0:T(8,128)(2,1)} %param.23, f32[512]{0:T(512)S(1)} %copy-done.15, pred[2048]{0:T(1024)(128)(4,1)S(1)} %get-tuple-element.3), kind=kOutput, calls=%fused_computation.21 | convolution fusion | flops 3226468352 | bytes 16257024 | tf_op jit(solution)/shard_map/dot_general | solution.py:74
  120.6 19.3 %scatter_custom_fusion.3 = f32[257,1024]{1,0:T(8,128)S(1)} fusion(s32[2048]{0:T(1024)S(1)} %bitcast.71, f32[2048,1024]{1,0:T(8,128)} %fusion.5, f32[]{:T(128)} %constant.46.clone.1), kind=kCustom, calls=%fused_computation.22 | custom fusion | flops 2097152 | bytes 1053184 | tf_op jit(solution)/shard_map/scatter-add | solution.py:75
  139.9 0.9 slice.101
  140.9 0.1 copy.49
  141.0 0.1 reshape.145
  141.1 0.1 copy.48
  141.2 0.6 fusion.1
  141.8 14.7 %scatter_custom_fusion.1 = f32[257]{0:T(512)S(1)} fusion(s32[2048]{0:T(1024)S(1)} %bitcast.72, f32[2048]{0:T(1024)S(1)} %get-tuple-element.2, f32[]{:T(128)} %constant.46.clone.1), kind=kCustom, calls=%fused_computation.83 | custom fusion | flops 2048 | bytes 1032 | tf_op jit(solution)/shard_map/scatter-add | solution.py:78
  156.5 14.1 %all-gather.3.cloned.1.call-done = bf16[1024,1024]{1,0:T(8,128)(2,1)} async-done(((bf16[256,1024]{1,0:T(8,128)(2,1)}), bf16[1024,1024]{1,0:T(8,128)(2,1)}) %all-gather.3.cloned.1.call-update) | async-done | bytes 2097168 | tf_op jit(solution)/shard_map/all_gather | solution.py:9
  170.5 2.9 %reduce_sum.34 = bf16[256,1024]{1,0:T(8,128)(2,1)} reduce(bf16[4,256,1024]{2,1,0:T(8,128)(2,1)} %bitcast.63, bf16[]{:T(256)} %constant.59.clone.1), dimensions={0}, to_apply=%region_7.8 | reduce | flops 786432 | bytes 2621442 | tf_op jit(solution)/shard_map/reduce_sum | solution.py:9
  173.5 2.2 fusion.2
  175.7 0.2 fusion.14
  175.9 7.5 %gather_fusion.1 = bf16[2048,256]{1,0:T(8,128)(2,1)S(1)} fusion(bf16[256,256]{1,0:T(8,128)(2,1)S(1)} %fusion.14, s32[2048]{0:T(1024)S(1)} %broadcast_clamp_fusion), kind=kCustom, calls=%fused_computation.1 | custom fusion | bytes 2105344 | tf_op jit(solution)/shard_map/jit(_take)/gather | solution.py:100
  183.4 1.3 broadcast_select_fusion
  184.7 10.6 %all-to-all-start.2 = ((bf16[64,32,256]{2,1,0:T(8,128)(2,1)}), bf16[64,32,256]{2,1,0:T(8,128)(2,1)S(1)}, u32[]{:S(2)}, u32[]{:S(2)}) async-start(bf16[64,32,256]{2,1,0:T(8,128)(2,1)} %broadcast_select_fusion), calls=%async_computation.2 | async-start | bytes 2097152 | tf_op jit(solution)/shard_map/all_to_all | solution.py:101
  195.3 0.3 reduce-scatter.2.cloned.1.call-start
  195.5 0.1 copy.50
  195.7 0.1 reshape.153
  195.8 0.1 copy.47
  196.0 1.2 gather_fusion.3
  197.2 26.8 %all-to-all-done.2 = bf16[64,32,256]{2,1,0:T(8,128)(2,1)S(1)} async-done(((bf16[64,32,256]{2,1,0:T(8,128)(2,1)}), bf16[64,32,256]{2,1,0:T(8,128)(2,1)S(1)}, u32[]{:S(2)}, u32[]{:S(2)}) %all-to-all-start.2) | async-done | bytes 1048608 | tf_op jit(solution)/shard_map/all_to_all | solution.py:101
  224.0 8.1 %gather_fusion.2 = bf16[2560,256]{1,0:T(8,128)(2,1)} fusion(bf16[2048,256]{1,0:T(8,128)(2,1)S(1)} %bitcast.60, s32[3072]{0:T(1024)S(1)} %pad_clamp_fusion), kind=kCustom, calls=%fused_computation.2 | custom fusion | bytes 2631680 | tf_op jit(solution)/shard_map/jit(_take)/gather | solution.py:103
  232.2 3.6 %reshape.152 = bf16[256,10,256]{2,1,0:T(8,128)(2,1)} reshape(bf16[2560,256]{1,0:T(8,128)(2,1)} %gather_fusion.2) | data formatting | bytes 2621440 | tf_op jit(solution)/shard_map/jit(_take)/gather | solution.py:103
  235.8 2.7 %convert_reduce_fusion = f32[256,256]{1,0:T(8,128)S(1)} fusion(bf16[256,10,256]{2,1,0:T(8,128)(2,1)} %reshape.152, pred[256,10]{1,0:T(8,128)(4,1)S(1)} %copy.47), kind=kLoop, calls=%fused_computation.8 | loop fusion | flops 1900544 | bytes 1575424 | tf_op jit(solution)/shard_map/reduce_sum | solution.py:104
  238.6 0.3 fusion.32
  238.9 1.1 fusion
  240.1 19.5 %reduce-scatter.2.cloned.1.call-done = bf16[64,1024]{1,0:T(8,128)(2,1)} async-done(((bf16[256,1024]{1,0:T(8,128)(2,1)}), bf16[64,1024]{1,0:T(8,128)(2,1)}) %reduce-scatter.2.cloned.1.call-update) | async-done | bytes 131088 | tf_op jit(solution)/shard_map/reduce_scatter | solution.py:106
  259.5 1.6 maximum_convert_fusion.1
  (52 shorter events, 0.3 us)
Async XLA Ops:
  7.2 134.0 %copy-start = (bf16[3,1024,256]{2,1,0:T(8,128)(2,1)S(1)}, bf16[3,1024,256]{2,1,0:T(8,128)(2,1)}, u32[]{:S(2)}) copy-start(bf16[3,1024,256]{2,1,0:T(8,128)(2,1)} %param.29) | copy-start | bytes 4718596
  7.2 19.4 %copy-start.8 = (s32[1024,1]{0,1:T(1,128)S(1)}, s32[1024,1]{0,1:T(1,128)}, u32[]{:S(2)}) copy-start(s32[1024,1]{0,1:T(1,128)} %param.20) | copy-start | bytes 12292
  31.9 20.7 %all-to-all-start = ((s32[64,1,32]{2,1,0:T(1,128)}), s32[64,1,32]{2,1,0:T(1,128)S(1)}, u32[]{:S(2)}, u32[]{:S(2)}) async-start(s32[64,1,32]{2,1,0:T(1,128)} %bitcast.6), calls=%async_computation | async-start | bytes 65536 | tf_op jit(solution)/shard_map/all_to_all | solution.py:60
  52.5 9.5 %copy-start.2 = (bf16[1024,512]{1,0:T(8,128)(2,1)S(1)}, bf16[1024,512]{1,0:T(8,128)(2,1)}, u32[]{:S(2)}) copy-start(bf16[1024,512]{1,0:T(8,128)(2,1)} %param.24) | copy-start | bytes 3145732
  52.5 60.4 %all-to-all-start.1 = ((bf16[64,32,512]{2,1,0:T(8,128)(2,1)}), bf16[64,32,512]{2,1,0:T(8,128)(2,1)}, u32[]{:S(2)}, u32[]{:S(2)}) async-start(bf16[64,32,512]{2,1,0:T(8,128)(2,1)} %bitcast.61), calls=%async_computation.1 | async-start | bytes 4194304 | tf_op jit(solution)/shard_map/all_to_all | solution.py:59
  61.8 108.8 %all-gather.3.cloned.1.call-start = ((), (), s32[]{:S(2)}) async-start(), calls=%async_computation.5 | async-start | bytes 2621440 | tf_op jit(solution)/shard_map/all_gather | solution.py:9
  64.9 48.0 %copy-start.11 = (bf16[512,1024]{1,0:T(8,128)(2,1)S(1)}, bf16[512,1024]{1,0:T(8,128)(2,1)}, u32[]{:S(2)}) copy-start(bf16[512,1024]{1,0:T(8,128)(2,1)} %param.26) | copy-start | bytes 3145732
  65.0 48.0 %copy-start.15 = (f32[512]{0:T(512)S(1)}, f32[512]{0:T(512)}, u32[]{:S(2)}) copy-start(f32[512]{0:T(512)} %param.25) | copy-start | bytes 6148
  120.6 20.2 %copy-start.6 = (s32[64,32]{0,1:T(8,128)S(1)}, s32[64,32]{0,1:T(8,128)}, u32[]{:S(2)}) copy-start(s32[64,32]{0,1:T(8,128)} %param.32) | copy-start | bytes 24580
  120.6 20.5 %copy-start.3 = (bf16[256,1024]{1,0:T(8,128)(2,1)S(1)}, bf16[256,1024]{1,0:T(8,128)(2,1)}, u32[]{:S(2)}) copy-start(bf16[256,1024]{1,0:T(8,128)(2,1)} %param.22) | copy-start | bytes 1572868
  120.6 20.5 %copy-start.12 = (f32[3,256]{1,0:T(4,128)S(1)}, f32[3,256]{1,0:T(4,128)}, u32[]{:S(2)}) copy-start(f32[3,256]{1,0:T(4,128)} %param.31) | copy-start | bytes 9220
  141.2 32.3 %copy-start.13 = (f32[1024]{0:T(1024)S(1)}, f32[1024]{0:T(1024)}, u32[]{:S(2)}) copy-start(f32[1024]{0:T(1024)} %param.27) | copy-start | bytes 12292
  141.2 32.3 %copy-start.14 = (f32[3,256]{1,0:T(4,128)S(1)}, f32[3,256]{1,0:T(4,128)}, u32[]{:S(2)}) copy-start(f32[3,256]{1,0:T(4,128)} %param.30) | copy-start | bytes 9220
  175.9 20.1 %copy-start.1 = (bf16[256,256]{1,0:T(8,128)(2,1)}, bf16[256,256]{1,0:T(8,128)(2,1)S(1)}, u32[]{:S(2)}) copy-start(bf16[256,256]{1,0:T(8,128)(2,1)S(1)} %fusion.14) | copy-start | bytes 393220
  183.4 12.1 %copy-start.7 = (s32[256,10]{0,1:T(8,128)S(1)}, s32[256,10]{0,1:T(8,128)}, u32[]{:S(2)}) copy-start(s32[256,10]{0,1:T(8,128)} %param.33) | copy-start | bytes 30724
  183.4 12.5 %copy-start.10 = (s32[256]{0:T(256)S(1)}, s32[256]{0:T(256)}, u32[]{:S(2)}) copy-start(s32[256]{0:T(256)} %param.34) | copy-start | bytes 3076
  184.7 39.3 %all-to-all-start.2 = ((bf16[64,32,256]{2,1,0:T(8,128)(2,1)}), bf16[64,32,256]{2,1,0:T(8,128)(2,1)S(1)}, u32[]{:S(2)}, u32[]{:S(2)}) async-start(bf16[64,32,256]{2,1,0:T(8,128)(2,1)} %broadcast_select_fusion), calls=%async_computation.2 | async-start | bytes 2097152 | tf_op jit(solution)/shard_map/all_to_all | solution.py:101
  195.3 64.3 %reduce-scatter.2.cloned.1.call-start = ((), (), s32[]{:S(2)}) async-start(), calls=%async_computation.4 | async-start | bytes 655360 | tf_op jit(solution)/shard_map/reduce_scatter | solution.py:106
  232.2 6.4 %copy-start.4 = (bf16[256,1024]{1,0:T(8,128)(2,1)S(1)}, bf16[256,1024]{1,0:T(8,128)(2,1)}, u32[]{:S(2)}) copy-start(bf16[256,1024]{1,0:T(8,128)(2,1)} %param.35) | copy-start | bytes 1572868
  235.8 3.1 %copy-start.5 = (bf16[256,1024]{1,0:T(8,128)(2,1)S(1)}, bf16[256,1024]{1,0:T(8,128)(2,1)}, u32[]{:S(2)}) copy-start(bf16[256,1024]{1,0:T(8,128)(2,1)} %param.36) | copy-start | bytes 1572868
  238.6 21.0 %copy-start.9 = (f32[1024]{0:T(1024)S(1)}, f32[1024]{0:T(1024)}, u32[]{:S(2)}) copy-start(f32[1024]{0:T(1024)} %param.37) | copy-start | bytes 12292
Sparse Core Ops, SparseCore 0:
  141.0 29.5 all-gather.2
  240.2 19.3 reduce-scatter.1
